TPU v7x, 512 devices: a whole 4x8x8 slice. The times are simulated.
512 devices in a mesh: req: 4 (over x), exp: 8 (over z), shard: 16 (over y, core).
Axes of the slice: x: 4, y: 8, z: 8, core: 2. Of those that a mesh axis runs over, the one named last changes fastest.
Arguments:
- query_stretch: bfloat16 [8, 128, 2304], P('req', 'exp'), may hold values from -8 to 8
- resid_stretch: bfloat16 [8, 128, 2304], P('req', 'exp'), may hold values from -30 to 30
- route_ids: int32 [8, 128, 2], P('req', 'exp'), may hold values from 0 to 7, all different within a row; in each aligned block of 16 rows (0 to 15, 16 to 31, ..., all dimensions but the last counted through in order) at most 6 rows name the same one
- route_probs: bfloat16 [8, 128, 2], P('req', 'exp'), may hold values from 0.19921875 to 1
- request_order: int32 [8], replicated, may hold values from 0 to 7, each once
- prior_pages: int32 [4, 2], P('req'), may hold values from 63 to 189, as said below
- page_order: int32 [4, 256], P('req'), may hold values from 0 to 255, each once within a row
- key_pool: bfloat16 [4, 256, 64, 2304], P('req', ('exp', 'shard')), may hold values from -8 to 8
- value_pool: bfloat16 [4, 256, 64, 2304], P('req', ('exp', 'shard')), may hold values from -6 to 6
- norm_gain: float32 [2304], replicated, may hold values from 0.4 to 2.5
- out_proj: bfloat16 [2304, 2304], P('shard'), may hold values from -0.125 to 0.125
- gate_up: bfloat16 [8, 2, 2880, 2304], P('exp', None, 'shard'), may hold values from -0.125 to 0.125
- down_proj: bfloat16 [8, 2880, 2304], P('exp', 'shard'), may hold values from -0.109375 to 0.109375
Outputs:
- mixed_out: bfloat16 [8, 128, 2304], P('req', 'exp')
Inputs may be any that keep to these rules, and one draw needn't show every extreme that they name: `route_ids`: each row names 2 different experts. In each aligned block of 16 rows (one request's tokens b * 16 to (b + 1) * 16 - 1) no expert is named by more than 6 rows, a bound that some block reaches. `request_order`: A permutation of the requests. `prior_pages`: in each group the 2 counts sum to 252, so that the pool is full; one member of every group has exactly 189. `page_order`: each row is a permutation of the group's pool pages.
All inputs are finite; a program needn't handle non-finite values.
Results may differ from a plain program's by a relative error of at most 0.02.
Values may be sent and summed in bfloat16 or wider, within the bound.
No kernel may reach another device: no remote copies, remote signals or barrier semaphores. Data moves between devices by JAX's collectives and lax.ppermute only.
A program may use at most 64 MiB of HBM per device.

v0:
```python
import math
import jax
import jax.numpy as jnp
from jax import lax
from jax.sharding import PartitionSpec as P

H = 36
NEG_FILL = -1e30
EPSILON = 1e-06


def expert_rows(received, gate_up, down_proj):
    width = received.shape[-1]
    flat_rows = received.reshape(-1, width)
    both = lax.dot_general(
        flat_rows, gate_up[0], (((1,), (2,)), ((), ())), preferred_element_type=jnp.float32
    )
    active = (jax.nn.silu(both[:, 0]) * both[:, 1]).astype(jnp.bfloat16)
    partial_out = jnp.dot(active, down_proj[0], preferred_element_type=jnp.float32)
    return partial_out.reshape(received.shape)


def on_device(
    query_stretch,
    resid_stretch,
    route_ids,
    route_probs,
    request_order,
    prior_pages,
    page_order,
    key_pool,
    value_pool,
    norm_gain,
    out_proj,
    gate_up,
    down_proj,
):
    members = prior_pages.shape[1]
    tokens_here = query_stretch.shape[1]
    width = query_stretch.shape[2]
    head_size = width // H
    group_index = lax.axis_index("req")
    exp_index = lax.axis_index("exp")
    shard_index = lax.axis_index("shard")
    shard_count = lax.axis_size("shard")
    experts_count = lax.axis_size("exp")
    all_query, all_resid, all_ids, all_probs = (
        lax.all_gather(query_stretch, "req", axis=0, tiled=True),
        lax.all_gather(resid_stretch, "req", axis=0, tiled=True),
        lax.all_gather(route_ids, "req", axis=0, tiled=True),
        lax.all_gather(route_probs, "req", axis=0, tiled=True),
    )
    served = lax.dynamic_slice_in_dim(request_order, group_index * members, members)
    served_query = jnp.take(all_query, served, axis=0)
    served_resid = jnp.take(all_resid, served, axis=0)
    served_ids = jnp.take(all_ids, served, axis=0)
    served_probs = jnp.take(all_probs, served, axis=0)
    group_query = lax.all_gather(served_query, "exp", axis=1, tiled=True)
    stretch_len = group_query.shape[1]
    pages_here = key_pool.shape[1]
    page_size = key_pool.shape[2]
    device_index = exp_index * shard_count + shard_index
    physical = device_index * pages_here + jnp.arange(pages_here, dtype=jnp.int32)
    page_row = page_order[0]
    pool_size = page_row.shape[0]
    matched = page_row[None, :] == physical[:, None]
    located = jnp.sum(
        jnp.where(matched, jnp.arange(pool_size, dtype=jnp.int32)[None, :], 0), axis=1
    )
    prior_row = prior_pages[0]
    page_counts = prior_row + stretch_len // page_size
    page_ends = jnp.cumsum(page_counts)
    page_starts = page_ends - page_counts
    owner_slot = jnp.sum((located[:, None] >= page_ends[None, :]).astype(jnp.int32), axis=1)
    owner_hot = owner_slot[:, None] == jnp.arange(members, dtype=jnp.int32)[None, :]
    logical = located - jnp.sum(jnp.where(owner_hot, page_starts[None, :], 0), axis=1)
    prior_here = jnp.sum(jnp.where(owner_hot, prior_row[None, :], 0), axis=1)
    key_place = logical[:, None] * page_size + jnp.arange(page_size, dtype=jnp.int32)[None, :]
    query_place = (
        prior_here[:, None] * page_size + jnp.arange(stretch_len, dtype=jnp.int32)[None, :]
    )
    visible = key_place[:, None, :] <= query_place[:, :, None]
    page_query = jnp.take(group_query, owner_slot, axis=0).reshape(
        pages_here, stretch_len, H, head_size
    )
    key_rows = key_pool[0].reshape(pages_here, page_size, H, head_size)
    value_rows = value_pool[0].reshape(pages_here, page_size, H, head_size)
    scores = jnp.einsum(
        "pqhd,pkhd->phqk", page_query, key_rows, preferred_element_type=jnp.float32
    ) * (1.0 / math.sqrt(head_size))
    scores = jnp.where(visible[:, None, :, :], scores, NEG_FILL)
    page_peak = jnp.max(scores, axis=3)
    local_peak = jnp.max(
        jnp.where(owner_hot[:, :, None, None], page_peak[:, None], NEG_FILL), axis=0
    )
    row_peak = lax.pmax(local_peak, ("exp", "shard"))
    peak_here = jnp.take(row_peak, owner_slot, axis=0)
    weights_bf = jnp.where(
        visible[:, None, :, :], jnp.exp(scores - peak_here[..., None]), 0.0
    ).astype(jnp.bfloat16)
    page_totals = jnp.sum(weights_bf, axis=3, dtype=jnp.float32)
    page_context = jnp.einsum(
        "phqk,pkhd->pqhd", weights_bf, value_rows, preferred_element_type=jnp.float32
    )
    page_context = page_context.reshape(pages_here, stretch_len, width)
    context = jnp.sum(jnp.where(owner_hot[:, :, None, None], page_context[:, None], 0.0), axis=0)
    totals = jnp.sum(jnp.where(owner_hot[:, :, None, None], page_totals[:, None], 0.0), axis=0)
    context_all, totals_all = lax.psum((context, totals), ("exp", "shard"))
    context_mine = lax.dynamic_slice_in_dim(context_all, exp_index * tokens_here, tokens_here, 1)
    totals_mine = lax.dynamic_slice_in_dim(totals_all, exp_index * tokens_here, tokens_here, 2)
    per_head = context_mine.reshape(members, tokens_here, H, head_size)
    attended = (
        (per_head / jnp.transpose(totals_mine, (0, 2, 1))[..., None])
        .reshape(members, tokens_here, width)
        .astype(jnp.bfloat16)
    )
    projected_part = lax.dot_general(
        attended, out_proj, (((2,), (1,)), ((), ())), preferred_element_type=jnp.float32
    ).astype(jnp.bfloat16)
    projected = lax.all_gather(projected_part, "shard", axis=2, tiled=True)
    hidden_state = served_resid.astype(jnp.float32) + projected.astype(jnp.float32)
    mean_square = jnp.mean(hidden_state * hidden_state, axis=2, keepdims=True)
    normed = (hidden_state * lax.rsqrt(mean_square + EPSILON) * norm_gain).astype(jnp.bfloat16)
    top_count = served_ids.shape[2]
    capacity = min(tokens_here, max(2, 3 * tokens_here * top_count // (2 * experts_count)))
    flat_ids = served_ids.reshape(members, tokens_here * top_count)
    expert_hot = (
        flat_ids[:, :, None] == jnp.arange(experts_count, dtype=jnp.int32)[None, None, :]
    ).astype(jnp.int32)
    before = jnp.cumsum(expert_hot, axis=1) - expert_hot
    slot_place = jnp.sum(before * expert_hot, axis=2)
    slot_hot = (
        slot_place[:, :, None] == jnp.arange(capacity, dtype=jnp.int32)[None, None, :]
    ).astype(jnp.int32)
    place_table = (expert_hot[:, :, :, None] * slot_hot[:, :, None, :]).reshape(
        members, tokens_here, top_count, experts_count, capacity
    )
    pick_table = jnp.sum(place_table, axis=2).astype(jnp.bfloat16)
    sent_rows = jnp.einsum(
        "jtnc,jtd->njcd", pick_table, normed, preferred_element_type=jnp.float32
    ).astype(jnp.bfloat16)
    share_table = jnp.sum(
        place_table.astype(jnp.bfloat16) * served_probs[:, :, :, None, None], axis=2
    )
    partial_out = expert_rows(
        lax.all_to_all(sent_rows, "exp", split_axis=0, concat_axis=0, tiled=True),
        gate_up,
        down_proj,
    )
    expert_out = lax.psum(partial_out.astype(jnp.bfloat16), "shard")
    returned = lax.all_to_all(expert_out, "exp", split_axis=0, concat_axis=0, tiled=True)
    moe_term = jnp.einsum(
        "jtnc,njcd->jtd", share_table, returned, preferred_element_type=jnp.float32
    )
    mixed_out = (hidden_state + moe_term).astype(jnp.bfloat16)
    return mixed_out


def solution(mesh):
    return jax.shard_map(
        on_device,
        mesh=mesh,
        in_specs=(
            P("req", "exp", None),
            P("req", "exp", None),
            P("req", "exp", None),
            P("req", "exp", None),
            P(),
            P("req", None),
            P("req", None),
            P("req", ("exp", "shard"), None, None),
            P("req", ("exp", "shard"), None, None),
            P(),
            P("shard", None),
            P("exp", None, "shard", None),
            P("exp", "shard", None),
        ),
        out_specs=P("req", "exp", None),
        check_vma=False,
    )
```

profile of v0, /device:TPU:1, one launch (start us, length us, event | category | flops | bytes accessed | tf_op | source)
XLA Modules:
  0.0 1259.9 jit_solution(11993732823770950947)
XLA Ops:
  7.4 11.4 all_gather.19
  20.2 8.2 all_gather.22
  32.6 2.8 reshape_squeeze.6
  36.9 10.4 all_gather.18
  47.8 18.5 %all-gather.2.cloned.1.call-done = bf16[2,128,2304]{2,1,0:T(8,128)(2,1)} async-done(((bf16[2,16,2304]{2,1,0:T(8,128)(2,1)}), bf16[2,128,2304]{2,1,0:T(8,128)(2,1)}) %all-gather.2.cloned.1.call-update) | async-done | bytes 1179664 | tf_op jit(solution)/shard_map/all_gather | solution.py:58
  66.3 1.9 gather_fusion
  68.2 1.4 copy.90
  69.6 3.8 fusion.3
  73.6 490.0 %pmax.7 = f32[2,36,128]{2,1,0:T(8,128)S(1)} all-reduce(f32[2,36,128]{2,1,0:T(8,128)S(1)} %copy.92), channel_id=1, replica_groups=mesh['req'=4,'exp'=8,'shard'=16] {'exp','shard'}, use_global_device_ids=true, to_apply=%region_7.9 | all-reduce | flops 9216 | bytes 73728 | tf_op jit(solution)/shard_map/pmax | solution.py:96
  564.2 3.7 fusion.32
  567.9 3.1 copy.94
  571.0 3.7 select_reduce_fusion
  576.4 2.4 convert_reduce_fusion
  578.9 491.2 %psum.22 = f32[2,36,128]{2,0,1:T(2,128)S(1)} all-reduce(f32[2,36,128]{2,0,1:T(2,128)S(1)} %select_reduce_fusion.1), channel_id=1, replica_groups=mesh['req'=4,'exp'=8,'shard'=16] {'exp','shard'}, use_global_device_ids=true, to_apply=%region_12.14 | all-reduce | flops 9216 | bytes 73728 | tf_op jit(solution)/shard_map/psum | solution.py:108
  1070.8 1.5 convolution_convert_fusion.2
  1072.4 23.8 %all_gather.21 = bf16[2,16,2304]{1,0,2:T(2,128)(2,1)S(1)} all-gather(bf16[2,16,144]{1,0,2:T(2,128)(2,1)S(1)} %copy.96), channel_id=1, replica_groups=mesh['req'=4,'exp'=8,'shard'=16] {'shard'}, dimensions={2}, use_global_device_ids=true | all-gather | bytes 156672 | tf_op jit(solution)/shard_map/all_gather | solution.py:120
  1096.3 1.4 copy.97
  1098.6 20.1 %all_to_all.10 = bf16[8,2,6,2304]{3,1,2,0:T(2,128)(2,1)S(1)} all-to-all(bf16[8,2,6,2304]{3,1,2,0:T(2,128)(2,1)S(1)} %copy.100), channel_id=1, replica_groups=mesh['req'=4,'exp'=8,'shard'=16] {'exp'}, dimensions={0} | all-to-all | bytes 884736 | tf_op jit(solution)/shard_map/all_to_all | solution.py:146
  1119.6 1.6 fusion.4
  1122.5 105.0 %all-reduce.5.cloned.1.call-done = bf16[8,2,6,2304]{3,0,2,1:T(8,128)(2,1)} async-done(((bf16[8,2,6,2304]{3,0,2,1:T(8,128)(2,1)}), bf16[8,2,6,2304]{3,0,2,1:T(8,128)(2,1)}) %all-reduce.5.cloned.1.call-update) | async-done | bytes 442384 | tf_op jit(solution)/shard_map/psum | solution.py:150
  1227.5 2.1 copy.105
  1229.6 6.7 all-to-all-start.1
  1236.3 7.9 all_gather.23
  1244.9 7.6 all-to-all-done.1
  (83 shorter events, 16.3 us)
Async XLA Ops:
  6.5 1113.1 %copy-start = (bf16[1,2,180,2304]{3,1,2,0:T(2,128)(2,1)S(1)}, bf16[1,2,180,2304]{3,1,2,0:T(2,128)(2,1)}, u32[]{:S(2)}) copy-start(bf16[1,2,180,2304]{3,1,2,0:T(2,128)(2,1)} %param.26) | copy-start | bytes 4976644
  6.5 28.8 %copy-start.3 = (bf16[1,2,64,2304]{3,2,1,0:T(8,128)(2,1)S(1)}, bf16[1,2,64,2304]{3,2,1,0:T(8,128)(2,1)}, u32[]{:S(2)}) copy-start(bf16[1,2,64,2304]{3,2,1,0:T(8,128)(2,1)} %param.23) | copy-start | bytes 1769476
  6.5 59.7 %all-gather.2.cloned.1.call-start = ((), (), s32[]{:S(2)}) async-start(), calls=%async_computation.2 | async-start | bytes 1327104 | tf_op jit(solution)/shard_map/all_gather | solution.py:58
  18.9 17.9 %copy-start.8 = (s32[1,2]{1,0:T(1,128)S(1)}, s32[1,2]{1,0:T(1,128)}, u32[]{:S(2)}) copy-start(s32[1,2]{1,0:T(1,128)} %param.20) | copy-start | bytes 28
  19.4 17.5 %copy-start.4 = (bf16[2,16,2304]{2,1,0:T(8,128)(2,1)S(1)}, bf16[2,16,2304]{2,1,0:T(8,128)(2,1)}, u32[]{:S(2)}) copy-start(bf16[2,16,2304]{2,1,0:T(8,128)(2,1)} %param.16) | copy-start | bytes 442372
  20.2 1050.6 %all-reduce.3.cloned.1.call-start = ((), (), s32[]{:S(2)}) async-start(), calls=%async_computation.3 | async-start | bytes 4718592 | tf_op jit(solution)/shard_map/psum | solution.py:108
  69.6 494.6 %copy-start.1 = (bf16[1,2,64,2304]{2,3,1,0:T(8,128)(2,1)S(1)}, bf16[1,2,64,2304]{2,3,1,0:T(8,128)(2,1)}, u32[]{:S(2)}) copy-start(bf16[1,2,64,2304]{2,3,1,0:T(8,128)(2,1)} %copy.110) | copy-start | bytes 1769476
  574.7 0.8 copy-start.5
  574.7 652.8 %all-reduce.5.cloned.1.call-start = ((), (), s32[]{:S(2)}) async-start(), calls=%async_computation.4 | async-start | bytes 884736 | tf_op jit(solution)/shard_map/psum | solution.py:150
  1070.7 27.2 %copy-start.6 = (f32[2304]{0:T(1024)S(1)}, f32[2304]{0:T(1024)}, u32[]{:S(2)}) copy-start(f32[2304]{0:T(1024)} %param.24) | copy-start | bytes 27652
  1118.7 2.8 copy-start.2
  1121.3 115.0 %copy-start.7 = (bf16[2,16,2]{1,2,0:T(2,128)(2,1)S(1)}, bf16[2,16,2]{1,2,0:T(2,128)(2,1)}, u32[]{:S(2)}) copy-start(bf16[2,16,2]{1,2,0:T(2,128)(2,1)} %param.18) | copy-start | bytes 388
  1229.6 22.9 %all-to-all-start.1 = ((bf16[8,2,6,2304]{3,1,2,0:T(2,128)(2,1)}), bf16[8,2,6,2304]{3,1,2,0:T(2,128)(2,1)S(1)}, u32[]{:S(2)}, u32[]{:S(2)}) async-start(bf16[8,2,6,2304]{3,1,2,0:T(2,128)(2,1)} %copy.105), calls=%async_computation.1 | async-start | bytes 884736 | tf_op jit(solution)/shard_map/all_to_all | solution.py:151
Sparse Core Ops, SparseCore 0:
  20.3 45.9 all-gather.1
  574.8 197.8 all-reduce.2
  1122.6 104.7 all-reduce.4
where the time goes:
time: 1260 us
  blocking collectives  1060 us (84%)
  waiting for transfers between devices  131 us (10%)
  local copies, waits for them, and re-layouts  20.2 us (2%)
  between operations  13.4 us (1%)
  matrix products  12.9 us (1%)
    psum x1, blocking collectives, on_device(): context_all, totals_all = lax.psum((context, totals), ('exp', 'shard'))  491 us
    pmax x1, blocking collectives, on_device(): row_peak = lax.pmax(local_peak, ('exp', 'shard'))  490 us
    psum x1, waiting for transfers between devices, on_device(): expert_out = lax.psum(partial_out.astype(jnp.bfloat16), 'shard')  105 us
  transfers between devices with their start and end apart: 4, of which 3 were waited for; matrix products, arithmetic and copies ran while one was open for 1% of the time, Pallas kernels for 0%

commit v1 on v0

--- a/solution.py
+++ b/solution.py
@@ -105,7 +105,7 @@
     page_context = page_context.reshape(pages_here, stretch_len, width)
     context = jnp.sum(jnp.where(owner_hot[:, :, None, None], page_context[:, None], 0.0), axis=0)
     totals = jnp.sum(jnp.where(owner_hot[:, :, None, None], page_totals[:, None], 0.0), axis=0)
-    context_all, totals_all = lax.psum((context, totals), ("exp", "shard"))
+    context_all, totals_all = lax.psum(lax.psum((context, totals), "shard"), "exp")
     context_mine = lax.dynamic_slice_in_dim(context_all, exp_index * tokens_here, tokens_here, 1)
     totals_mine = lax.dynamic_slice_in_dim(totals_all, exp_index * tokens_here, tokens_here, 2)
     per_head = context_mine.reshape(members, tokens_here, H, head_size)

time: 1260 us -> 989 us (0.78)
  blocking collectives: 1060 us -> 651 us
  waiting for transfers between devices: 131 us -> 274 us
    psum x1 -> x2, blocking collectives: 491 us -> 75.3 us  [the longest x1 50 us: on_device(): lax.psum((context, totals), 'shard')]
    psum x1 -> x2, waiting for transfers between devices: 0.02 us -> 119 us  [the longest x1 119 us: on_device(): lax.psum((context, totals), 'shard')]
    all_gather x1, waiting for transfers between devices: 18.5 us -> 39.5 us  [on_device(): group_query = lax.all_gather(served_query, 'exp', axis=1, tiled=True)]
  transfers between devices with their start and end apart: 4 -> 5, of which waited for: 3 -> 4; matrix products, arithmetic and copies ran while one was open for 1% -> 1% of each run, Pallas kernels for 0% -> 0%
where the time goes in v1:
time: 989 us
  blocking collectives  651 us (66%)
  waiting for transfers between devices  274 us (28%)
  local copies, waits for them, and re-layouts  19.4 us (2%)
  between operations  13.4 us (1%)
  matrix products  13 us (1%)
  other arithmetic  11.3 us (1%)
    pmax x1, blocking collectives, on_device(): row_peak = lax.pmax(local_peak, ('exp', 'shard'))  490 us
    psum x1, waiting for transfers between devices, on_device(): lax.psum((context, totals), 'shard')  119 us
    psum x1, waiting for transfers between devices, on_device(): expert_out = lax.psum(partial_out.astype(jnp.bfloat16), 'shard')  107 us
    psum x1, blocking collectives, on_device(): lax.psum((context, totals), 'shard')  50 us
    all_gather x1, waiting for transfers between devices, on_device(): group_query = lax.all_gather(served_query, 'exp', axis=1, tiled=True)  39.5 us
    all_gather x1, blocking collectives, on_device(): projected = lax.all_gather(projected_part, 'shard', axis=2, tiled=True)  27.8 us
    psum x1, blocking collectives, on_device(): lax.psum(lax.psum((context, totals), 'shard'), 'exp')  25.3 us
    all_to_all x1, blocking collectives, on_device(): lax.all_to_all(sent_rows, 'exp', split_axis=0, concat_axis=0, tiled=True)  20.3 us
  transfers between devices with their start and end apart: 5, of which 4 were waited for; matrix products, arithmetic and copies ran while one was open for 1% of the time, Pallas kernels for 0%

profile of v1, /device:TPU:1, one launch (start us, length us, event | category | flops | bytes accessed | tf_op | source)
XLA Modules:
  0.0 988.5 jit_solution(4497270542862573643)
XLA Ops:
  7.4 11.4 %all_gather.19 = bf16[8,16,2304]{2,1,0:T(8,128)(2,1)S(1)} all-gather(bf16[2,16,2304]{2,1,0:T(8,128)(2,1)} %param.15), channel_id=1, replica_groups=mesh['req'=4,'exp'=8,'shard'=16] {'req'}, dimensions={0}, use_global_device_ids=true | all-gather | bytes 737280 | tf_op jit(solution)/shard_map/all_gather | solution.py:48
  22.1 2.8 reshape_squeeze.6
  26.8 39.5 %all-gather.2.cloned.1.call-done = bf16[2,128,2304]{2,1,0:T(8,128)(2,1)} async-done(((bf16[2,16,2304]{2,1,0:T(8,128)(2,1)}), bf16[2,128,2304]{2,1,0:T(8,128)(2,1)}) %all-gather.2.cloned.1.call-update) | async-done | bytes 1179664 | tf_op jit(solution)/shard_map/all_gather | solution.py:58
  66.3 1.9 gather_fusion
  69.6 3.8 fusion.3
  73.6 489.8 %pmax.7 = f32[2,36,128]{2,1,0:T(8,128)S(1)} all-reduce(f32[2,36,128]{2,1,0:T(8,128)S(1)} %copy.92), channel_id=1, replica_groups=mesh['req'=4,'exp'=8,'shard'=16] {'exp','shard'}, use_global_device_ids=true, to_apply=%region_7.9 | all-reduce | flops 9216 | bytes 73728 | tf_op jit(solution)/shard_map/pmax | solution.py:96
  564.1 3.7 fusion.32
  567.8 3.0 copy.94
  570.8 3.8 select_reduce_fusion
  574.7 119.4 %all-reduce.4.cloned.1.call-done = f32[2,128,2304]{2,1,0:T(8,128)} async-done(((f32[2,128,2304]{2,1,0:T(8,128)}), f32[2,128,2304]{2,1,0:T(8,128)}) %all-reduce.4.cloned.1.call-update) | async-done | bytes 2359312 | tf_op jit(solution)/shard_map/psum | solution.py:108
  694.2 8.4 all_gather.22
  703.9 10.0 %all_gather.18 = bf16[8,16,2304]{2,1,0:T(8,128)(2,1)S(1)} all-gather(bf16[2,16,2304]{2,1,0:T(8,128)(2,1)S(1)} %copy-done.4), channel_id=1, replica_groups=mesh['req'=4,'exp'=8,'shard'=16] {'req'}, dimensions={0}, use_global_device_ids=true | all-gather | bytes 737280 | tf_op jit(solution)/shard_map/all_gather | solution.py:49
  714.6 2.4 convert_reduce_fusion
  717.1 50.0 %psum.37 = f32[2,36,128]{2,0,1:T(2,128)S(1)} all-reduce(f32[2,36,128]{2,0,1:T(2,128)S(1)} %select_reduce_fusion.1), channel_id=1, replica_groups=mesh['req'=4,'exp'=8,'shard'=16] {'shard'}, use_global_device_ids=true, to_apply=%region_13.15 | all-reduce | flops 9216 | bytes 73728 | tf_op jit(solution)/shard_map/psum | solution.py:108
  767.1 25.3 %psum.38 = f32[2,36,128]{2,0,1:T(2,128)S(1)} all-reduce(f32[2,36,128]{2,0,1:T(2,128)S(1)} %psum.37), channel_id=1, replica_groups=mesh['req'=4,'exp'=8,'shard'=16] {'exp'}, use_global_device_ids=true, to_apply=%region_14.16 | all-reduce | flops 9216 | bytes 73728 | tf_op jit(solution)/shard_map/psum | solution.py:108
  793.1 1.5 convolution_convert_fusion.2
  794.8 27.8 %all_gather.21 = bf16[2,16,2304]{1,0,2:T(2,128)(2,1)S(1)} all-gather(bf16[2,16,144]{1,0,2:T(2,128)(2,1)S(1)} %copy.96), channel_id=1, replica_groups=mesh['req'=4,'exp'=8,'shard'=16] {'shard'}, dimensions={2}, use_global_device_ids=true | all-gather | bytes 156672 | tf_op jit(solution)/shard_map/all_gather | solution.py:120
  824.9 20.3 %all_to_all.10 = bf16[8,2,6,2304]{3,1,2,0:T(2,128)(2,1)S(1)} all-to-all(bf16[8,2,6,2304]{3,1,2,0:T(2,128)(2,1)S(1)} %copy.100), channel_id=1, replica_groups=mesh['req'=4,'exp'=8,'shard'=16] {'exp'}, dimensions={0} | all-to-all | bytes 884736 | tf_op jit(solution)/shard_map/all_to_all | solution.py:146
  846.2 1.6 fusion.4
  849.1 107.0 %all-reduce.8.cloned.1.call-done = bf16[8,2,6,2304]{3,0,2,1:T(8,128)(2,1)} async-done(((bf16[8,2,6,2304]{3,0,2,1:T(8,128)(2,1)}), bf16[8,2,6,2304]{3,0,2,1:T(8,128)(2,1)}) %all-reduce.8.cloned.1.call-update) | async-done | bytes 442384 | tf_op jit(solution)/shard_map/psum | solution.py:150
  956.1 2.1 copy.105
  958.2 6.7 all-to-all-start.1
  964.9 7.9 all_gather.23
  973.5 7.6 all-to-all-done.1
  (87 shorter events, 17.3 us)
Async XLA Ops:
  6.5 839.6 %copy-start = (bf16[1,2,180,2304]{3,1,2,0:T(2,128)(2,1)S(1)}, bf16[1,2,180,2304]{3,1,2,0:T(2,128)(2,1)}, u32[]{:S(2)}) copy-start(bf16[1,2,180,2304]{3,1,2,0:T(2,128)(2,1)} %param.26) | copy-start | bytes 4976644
  6.5 18.4 %copy-start.3 = (bf16[1,2,64,2304]{3,2,1,0:T(8,128)(2,1)S(1)}, bf16[1,2,64,2304]{3,2,1,0:T(8,128)(2,1)}, u32[]{:S(2)}) copy-start(bf16[1,2,64,2304]{3,2,1,0:T(8,128)(2,1)} %param.23) | copy-start | bytes 1769476
  6.5 59.8 %all-gather.2.cloned.1.call-start = ((), (), s32[]{:S(2)}) async-start(), calls=%async_computation.2 | async-start | bytes 1327104 | tf_op jit(solution)/shard_map/all_gather | solution.py:58
  18.9 7.5 copy-start.8
  20.2 673.9 %all-reduce.4.cloned.1.call-start = ((), (), s32[]{:S(2)}) async-start(), calls=%async_computation.3 | async-start | bytes 4718592 | tf_op jit(solution)/shard_map/psum | solution.py:108
  69.6 494.4 %copy-start.1 = (bf16[1,2,64,2304]{2,3,1,0:T(8,128)(2,1)S(1)}, bf16[1,2,64,2304]{2,3,1,0:T(8,128)(2,1)}, u32[]{:S(2)}) copy-start(bf16[1,2,64,2304]{2,3,1,0:T(8,128)(2,1)} %copy.110) | copy-start | bytes 1769476
  574.6 119.6 %copy-start.6 = (s32[2,16,2]{1,2,0:T(2,128)S(1)}, s32[2,16,2]{1,2,0:T(2,128)}, u32[]{:S(2)}) copy-start(s32[2,16,2]{1,2,0:T(2,128)} %param.17) | copy-start | bytes 772
  574.6 129.3 %copy-start.4 = (bf16[2,16,2304]{2,1,0:T(8,128)(2,1)S(1)}, bf16[2,16,2304]{2,1,0:T(8,128)(2,1)}, u32[]{:S(2)}) copy-start(bf16[2,16,2304]{2,1,0:T(8,128)(2,1)} %param.16) | copy-start | bytes 442372
  574.6 218.5 %all-reduce.6.cloned.1.call-start = ((), (), s32[]{:S(2)}) async-start(), calls=%async_computation.4 | async-start | bytes 4718592 | tf_op jit(solution)/shard_map/psum | solution.py:108
  694.1 261.9 %all-reduce.8.cloned.1.call-start = ((), (), s32[]{:S(2)}) async-start(), calls=%async_computation.5 | async-start | bytes 884736 | tf_op jit(solution)/shard_map/psum | solution.py:150
  793.0 31.1 %copy-start.5 = (f32[2304]{0:T(1024)S(1)}, f32[2304]{0:T(1024)}, u32[]{:S(2)}) copy-start(f32[2304]{0:T(1024)} %param.24) | copy-start | bytes 27652
  845.2 2.8 copy-start.2
  847.8 117.1 %copy-start.7 = (bf16[2,16,2]{1,2,0:T(2,128)(2,1)S(1)}, bf16[2,16,2]{1,2,0:T(2,128)(2,1)}, u32[]{:S(2)}) copy-start(bf16[2,16,2]{1,2,0:T(2,128)(2,1)} %param.18) | copy-start | bytes 388
  958.2 22.9 %all-to-all-start.1 = ((bf16[8,2,6,2304]{3,1,2,0:T(2,128)(2,1)}), bf16[8,2,6,2304]{3,1,2,0:T(2,128)(2,1)S(1)}, u32[]{:S(2)}, u32[]{:S(2)}) async-start(bf16[8,2,6,2304]{3,1,2,0:T(2,128)(2,1)} %copy.105), calls=%async_computation.1 | async-start | bytes 884736 | tf_op jit(solution)/shard_map/all_to_all | solution.py:151
Sparse Core Ops, SparseCore 0:
  20.3 45.9 all-gather.1
  574.8 119.3 all-reduce.3
  696.5 87.6 all-reduce.5
  849.2 106.8 all-reduce.7
